TPU v7x, 512 devices: a whole 4x8x8 slice. The times are simulated.
512 devices in a mesh: row: 16 (over z, core), col: 32 (over x, y).
Axes of the slice: x: 4, y: 8, z: 8, core: 2. Of those that a mesh axis runs over, the one named last changes fastest.
Arguments:
- pool: float32 [131072, 256], P(('row', 'col')), may hold values from -12 to 12
- row_pick: int32 [65536], replicated, may hold values from 0 to 8191, as said below
- length_scale: float32 [256], replicated, may hold values from 12 to 48
- panel_tile: int32 [1], replicated, may hold values from 0 to 959
Outputs:
- schur: float32 [65536, 4096], P('row', 'col')
- row_panel: float32 [65536, 64], P('row')
Inputs may be any that keep to these rules, and one draw needn't show every extreme that they name: `row_pick`: entry m indexes the 8192 pixels of tile-grid row m // 4096; entries of one tile-grid row are distinct, at most 160 of them lie in the 256 pixels of one device, and exactly 160 do for some device of each tile-grid row.
All inputs are finite; a program needn't handle non-finite values.
Results may differ from a plain program's by a relative error of at most 0.0003.
Values sent between devices are 32-bit elements; how exact they have to be, the bound alone decides.
No kernel may reach another device: no remote copies, remote signals or barrier semaphores. Data moves between devices by JAX's collectives and lax.ppermute only.
A program may use at most 64 MiB of HBM per device.

v0:
```python
import jax
import jax.numpy as jnp
from jax import lax
from jax.sharding import PartitionSpec as P

TB = 64
WT = 2
noise_level = 0.1
root_five = 5.0**0.5


def from_root(x, axis, root):
    mine = lax.axis_index(axis) == root
    return lax.psum(jnp.where(mine, x, jnp.zeros_like(x)), axis)


def kernel(left, right, left_index, right_index):
    left_sq = jnp.sum(left * left, axis=1)
    right_sq = jnp.sum(right * right, axis=1)
    cross = jnp.dot(
        left, right.T, precision=lax.Precision.HIGHEST, preferred_element_type=jnp.float32
    )
    dist_sq = jnp.maximum(left_sq[:, None] + right_sq[None, :] - 2.0 * cross, 0.0)
    radius = jnp.sqrt(dist_sq)
    value = (1.0 + root_five * radius + 5.0 / 3.0 * dist_sq) * jnp.exp(-root_five * radius)
    same = (left_index[:, None] == right_index[None, :]).astype(value.dtype)
    return value + noise_level * same


def panel_solve(factor, block):
    return lax.linalg.triangular_solve(factor, block, left_side=False, lower=True, transpose_a=True)


def body(pool, row_pick, length_scale, panel_tile):
    rows_count = lax.axis_size("row")
    cols_count = lax.axis_size("col")
    my_row = lax.axis_index("row")
    my_col = lax.axis_index("col")
    total_rows = row_pick.shape[0]
    local_rows = total_rows // rows_count
    my_pick = lax.dynamic_slice_in_dim(row_pick, my_row * local_rows, local_rows)
    gathered = lax.all_gather(pool, "col", axis=0, tiled=True)
    features = jnp.take(gathered, my_pick, axis=0)
    panel = panel_tile[0]
    tiles = panel + 1 + jnp.mod(my_col - panel - 1, cols_count) + cols_count * jnp.arange(WT)
    local_tiles = tiles // rows_count
    col_source = (local_tiles[:, None] * TB + jnp.arange(TB)[None, :]).reshape(-1)
    col_local = jnp.take(features, col_source, axis=0)
    col_feats = from_root(col_local, "row", my_col % rows_count)
    panel_row = panel % rows_count
    panel_local = panel // rows_count
    panel_rows = lax.dynamic_slice_in_dim(features, panel_local * TB, TB)
    panel_feats = from_root(panel_rows, "row", panel_row)
    inverse_scale = 1.0 / length_scale
    scaled_rows = features * inverse_scale
    scaled_cols = col_feats * inverse_scale
    scaled_panel = panel_feats * inverse_scale
    local_index = jnp.arange(local_rows)
    row_global = (local_index // TB * rows_count + my_row) * TB + local_index % TB
    col_global = (tiles[:, None] * TB + jnp.arange(TB)[None, :]).reshape(-1)
    panel_global = panel * TB + jnp.arange(TB)
    factor = jnp.linalg.cholesky(kernel(scaled_panel, scaled_panel, panel_global, panel_global))
    row_panel = panel_solve(factor, kernel(scaled_rows, scaled_panel, row_global, panel_global))
    col_panel = panel_solve(factor, kernel(scaled_cols, scaled_panel, col_global, panel_global))
    update = jnp.dot(
        row_panel, col_panel.T, precision=lax.Precision.HIGHEST, preferred_element_type=jnp.float32
    )
    schur = kernel(scaled_rows, scaled_cols, row_global, col_global) - update
    return (schur, row_panel)


def solution(mesh):
    in_specs = (P(("row", "col"), None), P(), P(), P())
    out_specs = (P("row", "col"), P("row", None))
    return jax.shard_map(body, mesh=mesh, in_specs=in_specs, out_specs=out_specs, check_vma=False)
```

profile of v0, /device:TPU:1, one launch (start us, length us, event | category | flops | bytes accessed | tf_op | source)
XLA Modules:
  0.0 298.0 jit_solution(12258355929983849131)
XLA Ops:
  7.2 0.7 all-gather.2.cloned.1.call-update
  9.1 0.7 compare_and_fusion
  9.8 0.7 fusion.75
  10.5 0.7 broadcast_divide_fusion
  11.2 107.6 %all-gather.2.cloned.1.call-done = f32[8192,256]{1,0:T(8,128)} async-done(((f32[256,256]{1,0:T(8,128)}), f32[8192,256]{1,0:T(8,128)}) %all-gather.2.cloned.1.call-update) | async-done | bytes 8388624 | tf_op jit(solution)/shard_map/all_gather | solution.py:42
  118.9 19.5 %gather_fusion = f32[4096,256]{1,0:T(8,128)} fusion(f32[8192,256]{1,0:T(8,128)} %all-gather.2.cloned.1.call-done, s32[4096]{0:T(1024)S(1)} %fusion.75), kind=kCustom, calls=%fused_computation | custom fusion | bytes 8404992 | tf_op jit(solution)/shard_map/jit(_take)/gather | solution.py:43
  138.3 4.1 %multiply_reduce_fusion = (f32[4096]{0:T(1024)S(1)}, f32[4096,256]{1,0:T(8,128)}) fusion(f32[256]{0:T(256)S(1)} %broadcast_divide_fusion, f32[4096,256]{1,0:T(8,128)} %gather_fusion, pred[4096]{0:T(1024)(128)(4,1)S(1)} %compare_and_fusion), kind=kLoop, calls=%fused_computation.9 | loop fusion | flops 4190208 | bytes 8410112 | tf_op jit(solution)/shard_map/reduce_sum | solution.py:18
  142.4 2.9 gather_fusion.1
  145.4 1.5 dynamic-slice_select_fusion
  146.8 0.7 select_select_fusion
  147.6 110.7 %all-reduce.3.cloned.1.call-done = (f32[64,256]{1,0:T(8,128)}, f32[128,256]{1,0:T(8,128)}) async-done(((f32[64,256]{1,0:T(8,128)}, f32[128,256]{1,0:T(8,128)}), (f32[64,256]{1,0:T(8,128)}, f32[128,256]{1,0:T(8,128)})) %all-reduce.3.cloned.1.call-update) | async-done | bytes 196624 | tf_op jit(solution)/shard_map/psum | solution.py:14
  258.3 0.9 multiply_reduce_fusion.2
  259.3 1.1 fusion.91
  260.5 6.6 %fusion.3 = f32[4096,64]{0,1:T(8,128)S(1)} fusion(f32[4096,256]{1,0:T(8,128)} %get-tuple-element.7, f32[256]{0:T(256)S(1)} %broadcast_divide_fusion, f32[64]{0:T(128)S(1)} %multiply_reduce_fusion.2, f32[4096]{0:T(1024)S(1)} %get-tuple-element.6, f32[64,256]{1,0:T(8,128)} %get-tuple-element.2), kind=kOutput, calls=%fused_computation.8 | convolution fusion | flops 807419904 | bytes 5326080 | tf_op jit(solution)/shard_map/dot_general | solution.py:20
  267.1 0.1 multiply_reduce_fusion.1
  267.2 0.3 fusion.9
  267.5 3.4 %fusion.1 = f32[4096,128]{1,0:T(8,128)S(1)} fusion(f32[4096,256]{1,0:T(8,128)S(1)} %copy-done, f32[256]{0:T(256)S(1)} %broadcast_divide_fusion, f32[128]{0:T(128)S(1)} %multiply_reduce_fusion.1, f32[4096]{0:T(1024)S(1)} %get-tuple-element.6, f32[128,256]{1,0:T(8,128)S(1)} %copy-done.1), kind=kOutput, calls=%fused_computation.5 | convolution fusion | flops 1613791232 | bytes 6440448 | tf_op jit(solution)/shard_map/dot_general | solution.py:20
  271.3 5.8 %cholesky.15 = f32[64,64]{1,0:T(8,128)S(1)} custom-call(f32[64,64]{1,0:T(8,128)S(1)} %add_multiply_fusion), custom_call_target="Cholesky" | custom-call | tf_op jit(solution)/shard_map/jit(cholesky)/cholesky | solution.py:62
  277.2 0.6 compare_reduce_fusion
  277.8 0.7 fusion.37
  278.5 4.9 %custom-call.8 = f32[1,64,64]{1,2,0:T(8,128)S(1)} custom-call(f32[1,64,64]{2,1,0:T(8,128)S(1)} %fusion.37), custom_call_target="InvertDiagBlocksLowerTriangular" | custom-call | tf_op jit(solution)/shard_map/triangular_solve | solution.py:31
  283.4 1.7 fusion.10
  285.1 0.4 fusion.38
  285.5 5.7 %convolution_subtract_fusion = f32[4096,128]{1,0:T(8,128)} fusion(f32[4096,64]{0,1:T(8,128)S(1)} %fusion.10, f32[128,64]{1,0:T(8,128)S(1)} %fusion.38, f32[4096,128]{1,0:T(8,128)S(1)} %fusion.1, s32[128]{0:T(128)S(1)} %add.328, s32[4096]{0:T(1024)S(1)} %fusion.65), kind=kOutput, calls=%fused_computation.2 | convolution fusion | flops 407896064 | bytes 5292544 | tf_op jit(solution)/shard_map/dot_general | solution.py:65
  (27 shorter events, 0.9 us)
Async XLA Ops:
  7.2 111.7 %all-gather.2.cloned.1.call-start = ((), (), s32[]{:S(2)}) async-start(), calls=%async_computation | async-start | bytes 8650752 | tf_op jit(solution)/shard_map/all_gather | solution.py:42
  7.9 250.4 %all-reduce.3.cloned.1.call-start = ((), (), s32[]{:S(2)}) async-start(), calls=%async_computation.1 | async-start | bytes 393216 | tf_op jit(solution)/shard_map/psum | solution.py:14
  260.4 6.7 %copy-start.1 = (f32[128,256]{1,0:T(8,128)S(1)}, f32[128,256]{1,0:T(8,128)}, u32[]{:S(2)}) copy-start(f32[128,256]{1,0:T(8,128)} %get-tuple-element.3) | copy-start | bytes 393220
  260.4 6.8 %copy-start.2 = (f32[64,256]{1,0:T(8,128)S(1)}, f32[64,256]{1,0:T(8,128)}, u32[]{:S(2)}) copy-start(f32[64,256]{1,0:T(8,128)} %get-tuple-element.2) | copy-start | bytes 196612
  260.5 7.0 %copy-start = (f32[4096,256]{1,0:T(8,128)S(1)}, f32[4096,256]{1,0:T(8,128)}, u32[]{:S(2)}) copy-start(f32[4096,256]{1,0:T(8,128)} %get-tuple-element.7) | copy-start | bytes 12582916
  285.1 6.0 %copy-start.3 = (f32[4096,64]{0,1:T(8,128)}, f32[4096,64]{0,1:T(8,128)S(1)}, u32[]{:S(2)}) copy-start(f32[4096,64]{0,1:T(8,128)S(1)} %fusion.10) | copy-start | bytes 3145732
Sparse Core Ops, SparseCore 0:
  11.1 107.6 all-gather.1
  147.7 110.5 all-reduce.2
where the time goes:
time: 298 us
  waiting for transfers between devices  219 us (73%)
  local copies, waits for them, and re-layouts  22.9 us (8%)
  other arithmetic  21.9 us (7%)
  matrix products  19.2 us (6%)
  between operations  14.9 us (5%)
    psum x1, waiting for transfers between devices, from_root(): return lax.psum(jnp.where(mine, x, jnp.zeros_like(x)), axis)  111 us
    all_gather x1, waiting for transfers between devices, body(): gathered = lax.all_gather(pool, 'col', axis=0, tiled=True)  108 us
    gather x1, local copies, waits for them, and re-layouts, body(): features = jnp.take(gathered, my_pick, axis=0)  19.5 us
    dot_general x4, matrix products, kernel(): jnp.dot(left, right.T, precision=lax.Precision.HIGHEST, preferred_element...  11.5 us
    another operation x3, other arithmetic, body(): jnp.linalg.cholesky(kernel(scaled_panel, scaled_panel, panel_global, pane...  6.52 us
  transfers between devices with their start and end apart: 2, of which 2 were waited for; matrix products, arithmetic and copies ran while one was open for 1% of the time, Pallas kernels for 0%

commit v1 on v0

--- a/solution.py
+++ b/solution.py
@@ -11,7 +11,7 @@
 
 def from_root(x, axis, root):
     mine = lax.axis_index(axis) == root
-    return lax.psum(jnp.where(mine, x, jnp.zeros_like(x)), axis)
+    return jnp.sum(lax.all_gather(jnp.where(mine, x, jnp.zeros_like(x)), axis), axis=0)
 
 
 def kernel(left, right, left_index, right_index):

time: 298 us -> 249 us (0.84)
  waiting for transfers between devices: 219 us -> 167 us
    psum x1 -> x0, waiting for transfers between devices: 111 us -> none  [from_root(): return lax.psum(jnp.where(mine, x, jnp.zeros_like(x)), axis)]
    all_gather x0 -> x2, waiting for transfers between devices: none -> 57.9 us  [from_root(): lax.all_gather(jnp.where(mine, x, jnp.zeros_like(x)), axis)]
    reduce_sum x0 -> x2, other arithmetic: none -> 3.02 us  [from_root(): jnp.sum(lax.all_gather(jnp.where(mine, x, jnp.zeros_like(x)), axis), axis=0)]
  transfers between devices with their start and end apart: 2 -> 3, of which waited for: 2 -> 3; matrix products, arithmetic and copies ran while one was open for 1% -> 11% of each run, Pallas kernels for 0% -> 0%
where the time goes in v1:
time: 249 us; the launch traced here: 248 us
  waiting for transfers between devices  167 us (67%)
  local copies, waits for them, and re-layouts  24.8 us (10%)
  other arithmetic  22 us (9%)
  matrix products  19.9 us (8%)
  between operations  14.6 us (6%)
    all_gather x1, waiting for transfers between devices, body(): gathered = lax.all_gather(pool, 'col', axis=0, tiled=True)  108 us
    all_gather x2, waiting for transfers between devices, from_root(): lax.all_gather(jnp.where(mine, x, jnp.zeros_like(x)), axis)  57.9 us
    gather x1, local copies, waits for them, and re-layouts, body(): features = jnp.take(gathered, my_pick, axis=0)  19.5 us
    dot_general x4, matrix products, kernel(): jnp.dot(left, right.T, precision=lax.Precision.HIGHEST, preferred_element...  12.3 us
    another operation x3, other arithmetic, body(): jnp.linalg.cholesky(kernel(scaled_panel, scaled_panel, panel_global, pane...  6.52 us
    dot_general x1, matrix products, body(): jnp.dot(row_panel, col_panel.T, precision=lax.Precision.HIGHEST, preferre...  5.67 us
    another operation x2, other arithmetic, panel_solve(): lax.linalg.triangular_solve(factor, block, left_side=False, lower=True, t...  5.57 us
  transfers between devices with their start and end apart: 3, of which 3 were waited for; matrix products, arithmetic and copies ran while one was open for 11% of the time, Pallas kernels for 0%

profile of v1, /device:TPU:1, one launch (start us, length us, event | category | flops | bytes accessed | tf_op | source)
XLA Modules:
  0.0 248.1 jit_solution(2899267176634873931)
XLA Ops:
  7.2 0.7 all-gather.5.cloned.1.call-update
  8.6 0.7 compare_and_fusion
  9.4 0.7 fusion.76
  10.1 0.7 broadcast_divide_fusion
  10.8 108.1 %all-gather.5.cloned.1.call-done = f32[8192,256]{1,0:T(8,128)} async-done(((f32[256,256]{1,0:T(8,128)}), f32[8192,256]{1,0:T(8,128)}) %all-gather.5.cloned.1.call-update) | async-done | bytes 8388624 | tf_op jit(solution)/shard_map/all_gather | solution.py:42
  118.9 19.5 %gather_fusion = f32[4096,256]{1,0:T(8,128)} fusion(f32[8192,256]{1,0:T(8,128)} %all-gather.5.cloned.1.call-done, s32[4096]{0:T(1024)S(1)} %fusion.76), kind=kCustom, calls=%fused_computation | custom fusion | bytes 8404992 | tf_op jit(solution)/shard_map/jit(_take)/gather | solution.py:43
  138.3 2.9 %multiply_reduce_fusion = (f32[4096]{0:T(1024)S(1)}, f32[4096,256]{1,0:T(8,128)S(1)}) fusion(f32[256]{0:T(256)S(1)} %broadcast_divide_fusion, f32[4096,256]{1,0:T(8,128)} %gather_fusion, pred[4096]{0:T(1024)(128)(4,1)S(1)} %compare_and_fusion), kind=kLoop, calls=%fused_computation.9 | loop fusion | flops 4190208 | bytes 8410112 | tf_op jit(solution)/shard_map/reduce_sum | solution.py:18
  141.2 1.9 copy-done
  143.1 0.6 dynamic-slice_select_fusion
  144.2 2.9 %gather_fusion.1 = f32[128,256]{1,0:T(8,128)S(1)} fusion(f32[4096,256]{1,0:T(8,128)} %copy-done, s32[1024]{0:T(1024)S(1)} %pad_clamp_fusion), kind=kCustom, calls=%fused_computation.1 | custom fusion | bytes 262656 | tf_op jit(solution)/shard_map/jit(_take)/gather | solution.py:48
  147.1 0.7 fusion.30
  148.0 36.5 %all-gather.9.cloned.1.call-done = f32[1024,256]{1,0:T(8,128)} async-done(((f32[64,256]{1,0:T(8,128)}), f32[1024,256]{1,0:T(8,128)}) %all-gather.9.cloned.1.call-update) | async-done | bytes 1048592 | tf_op jit(solution)/shard_map/all_gather | solution.py:14
  184.5 1.3 reduce_sum.49
  186.5 5.8 %cholesky.15 = f32[64,64]{1,0:T(8,128)S(1)} custom-call(f32[64,64]{1,0:T(8,128)S(1)} %add_multiply_fusion), custom_call_target="Cholesky" | custom-call | tf_op jit(solution)/shard_map/jit(cholesky)/cholesky | solution.py:62
  192.4 0.6 compare_reduce_fusion
  193.0 0.7 fusion.38
  193.7 4.9 %custom-call.8 = f32[1,64,64]{1,2,0:T(8,128)S(1)} custom-call(f32[1,64,64]{2,1,0:T(8,128)S(1)} %fusion.38), custom_call_target="InvertDiagBlocksLowerTriangular" | custom-call | tf_op jit(solution)/shard_map/triangular_solve | solution.py:31
  198.6 6.5 %fusion.3 = f32[4096,64]{0,1:T(8,128)S(1)} fusion(f32[4096,256]{1,0:T(8,128)} %copy-done, f32[256]{0:T(256)S(1)} %broadcast_divide_fusion, f32[64]{0:T(128)S(1)} %multiply_reduce_fusion.2, f32[4096]{0:T(1024)S(1)} %get-tuple-element.4, f32[64,256]{1,0:T(8,128)S(1)} %reduce_sum.49), kind=kOutput, calls=%fused_computation.8 | convolution fusion | flops 807419904 | bytes 5326080 | tf_op jit(solution)/shard_map/dot_general | solution.py:20
  205.1 1.7 fusion.10
  206.8 21.4 %all-gather.7.cloned.1.call-done = f32[16,128,256]{2,1,0:T(8,128)} async-done(((f32[1,128,256]{2,1,0:T(8,128)}), f32[16,128,256]{2,1,0:T(8,128)}) %all-gather.7.cloned.1.call-update) | async-done | bytes 2097168 | tf_op jit(solution)/shard_map/all_gather | solution.py:14
  228.2 1.7 reduce_sum.44
  230.1 0.3 fusion.9
  230.3 5.3 %fusion.1 = f32[4096,128]{1,0:T(8,128)S(1)} fusion(f32[4096,256]{1,0:T(8,128)} %copy-done, f32[256]{0:T(256)S(1)} %broadcast_divide_fusion, f32[128]{0:T(128)S(1)} %multiply_reduce_fusion.1, f32[4096]{0:T(1024)S(1)} %get-tuple-element.4, f32[128,256]{1,0:T(8,128)S(1)} %reduce_sum.44), kind=kOutput, calls=%fused_computation.5 | convolution fusion | flops 1613791232 | bytes 6440448 | tf_op jit(solution)/shard_map/dot_general | solution.py:20
  235.9 5.7 %convolution_subtract_fusion = f32[4096,128]{1,0:T(8,128)} fusion(f32[4096,64]{0,1:T(8,128)S(1)} %fusion.10, f32[128,64]{0,1:T(8,128)S(1)} %fusion.39, f32[4096,128]{1,0:T(8,128)S(1)} %fusion.1, s32[128]{0:T(128)S(1)} %add.324, s32[4096]{0:T(1024)S(1)} %fusion.66), kind=kOutput, calls=%fused_computation.2 | convolution fusion | flops 407896064 | bytes 5292544 | tf_op jit(solution)/shard_map/dot_general | solution.py:65
  (28 shorter events, 1.6 us)
Async XLA Ops:
  7.2 111.7 %all-gather.5.cloned.1.call-start = ((), (), s32[]{:S(2)}) async-start(), calls=%async_computation | async-start | bytes 8650752 | tf_op jit(solution)/shard_map/all_gather | solution.py:42
  7.9 176.6 %all-gather.9.cloned.1.call-start = ((), (), s32[]{:S(2)}) async-start(), calls=%async_computation.2 | async-start | bytes 1114112 | tf_op jit(solution)/shard_map/all_gather | solution.py:14
  141.2 1.9 copy-start
  143.8 84.4 %all-gather.7.cloned.1.call-start = ((), (), s32[]{:S(2)}) async-start(), calls=%async_computation.1 | async-start | bytes 2228224 | tf_op jit(solution)/shard_map/all_gather | solution.py:14
  206.8 29.1 %copy-start.1 = (f32[4096,64]{0,1:T(8,128)}, f32[4096,64]{0,1:T(8,128)S(1)}, u32[]{:S(2)}) copy-start(f32[4096,64]{0,1:T(8,128)S(1)} %fusion.10) | copy-start | bytes 3145732
Sparse Core Ops, SparseCore 0:
  11.1 107.6 all-gather.4
  143.9 40.5 all-gather.8
  187.2 40.9 all-gather.6
